TPU v7x, 256 devices: a whole 4x4x8 slice. The times are simulated.
256 devices in a mesh: req: 4 (over x), tp: 64 (over z, y, core).
Axes of the slice: x: 4, y: 4, z: 8, core: 2. Of those that a mesh axis runs over, the one named last changes fastest.
Arguments:
- hidden: bfloat16 [256, 4096], P('req', 'tp'), may hold values from -6 to 6
- norm_gain: bfloat16 [4096], P('tp'), may hold values from 0.099609375 to 1.8984375
- w_qkv: bfloat16 [4096, 5120], P('tp'), may hold values from -0.1875 to 0.1875
- w_out: bfloat16 [4096, 4096], P('tp'), may hold values from -0.09375 to 0.09375
- cache_keys: bfloat16 [4, 65536, 512], P('req', 'tp')
- cache_values: bfloat16 [4, 65536, 512], P('req', 'tp'), may hold values from -6 to 6
- parents: int32 [4, 64], P('req'), may hold values from -1 to 62, as said below
- draft_counts: int32 [4], P('req'), may hold values from 1 to 64, as said below
- cache_lengths: int32 [4], P('req'), may hold values from 1 to 65536, as said below
Outputs:
- updated: bfloat16 [256, 4096], P('req', 'tp')
Inputs may be any that keep to these rules, and one draw needn't show every extreme that they name: parents[r, 0] = -1 and 0 <= parents[r, i] < i for i >= 1. `draft_counts`: some request has all 64 tree tokens live. `cache_lengths`: some request has a full cache of 65536 positions.
All inputs are finite; a program needn't handle non-finite values.
Results may differ from a plain program's by a relative error of at most 0.0065.
The roundings to bfloat16 on the way count: a program that leaves them out, or rounds other values in their place, can miss the bound.
Values may be sent and summed in bfloat16 or wider, within the bound.
No kernel may reach another device: no remote copies, remote signals or barrier semaphores. Data moves between devices by JAX's collectives and lax.ppermute only.
A program may use at most 64 MiB of HBM per device.

v0:
```python
import jax
import jax.numpy as jnp
from jax import lax
from jax.sharding import PartitionSpec as P

HEADS = 32
KV_HEADS = 4
HEAD = 128
NEGATIVE = -1e30


def tree_reach(parents):
    width = parents.shape[1]
    places = jnp.arange(width, dtype=jnp.int32)
    parent_link = (parents[:, :, None] == places[None, None, :]).astype(jnp.float32)
    identity = (places[:, None] == places[None, :]).astype(jnp.float32)
    reached = jnp.minimum(parent_link + identity[None], 1.0)
    for rounds in range(width.bit_length()):
        reached = jnp.minimum(
            jnp.einsum("rij,rjk->rik", reached, reached, precision=lax.Precision.HIGHEST), 1.0
        )
    return reached


def on_device(
    hidden, norm_gain, w_qkv, w_out, cache_keys, cache_values, parents, draft_counts, cache_lengths
):
    tp_count = lax.axis_size("tp")
    tp_rank = lax.axis_index("tp")
    model_width = w_out.shape[1]
    kv_width = KV_HEADS * HEAD
    groups = HEADS // KV_HEADS
    tree = parents.shape[1]
    requests = cache_keys.shape[0]
    places_dev = cache_keys.shape[1]
    inputs = hidden.astype(jnp.float32)
    all_rows = inputs.shape[0]
    own_count = all_rows // tp_count
    scaled = (inputs * norm_gain.astype(jnp.float32)[None, :]).astype(jnp.bfloat16)
    local_squares = jnp.sum(inputs * inputs, axis=1)
    raw, square_sum = lax.psum(
        (jnp.dot(scaled, w_qkv, preferred_element_type=jnp.float32), local_squares), "tp"
    )
    qkv = (raw * lax.rsqrt(square_sum / model_width + 1e-05)[:, None]).astype(jnp.bfloat16)
    query = qkv[:, :model_width]
    own_tokens = lax.dynamic_slice_in_dim(qkv, tp_rank * own_count, own_count, 0)[:, model_width:]
    own_keys = own_tokens[:, :kv_width].reshape(own_count, KV_HEADS, HEAD)
    own_values = own_tokens[:, kv_width:].reshape(own_count, KV_HEADS, HEAD)
    scale = HEAD ** (-0.5)
    key_index = tp_rank * own_count + jnp.arange(own_count, dtype=jnp.int32)
    key_request = key_index // tree
    key_place = key_index % tree
    query_request = jnp.arange(all_rows, dtype=jnp.int32) // tree
    reached = tree_reach(parents).reshape(all_rows, tree)
    column_pick = (jnp.arange(tree, dtype=jnp.int32)[:, None] == key_place[None, :]).astype(
        jnp.float32
    )
    on_path = jnp.dot(reached, column_pick, precision=lax.Precision.HIGHEST) > 0.5
    request_pick = jnp.arange(requests, dtype=jnp.int32)[:, None] == key_request[None, :]
    key_count = jnp.sum(jnp.where(request_pick, draft_counts[:, None], 0), axis=0)
    tree_mask = (
        on_path
        & (query_request[:, None] == key_request[None, :])
        & (key_place < key_count)[None, :]
    )
    query_heads = query.reshape(all_rows, KV_HEADS, groups, HEAD)
    query_blocks = query.reshape(requests, tree, KV_HEADS, groups, HEAD)
    first_place = tp_rank * places_dev
    positions = first_place + jnp.arange(places_dev, dtype=jnp.int32)

    def cache_scores(items):
        queries, keys, length = items
        scores = (
            jnp.einsum(
                "tkgd,pkd->tkgp",
                queries,
                keys.reshape(places_dev, KV_HEADS, HEAD),
                preferred_element_type=jnp.float32,
            )
            * scale
        )
        return jnp.where((positions < length)[None, None, None, :], scores, NEGATIVE)

    stored_scores = lax.map(cache_scores, (query_blocks, cache_keys, cache_lengths))
    tree_scores = (
        jnp.einsum("tkgd,ukd->tkgu", query_heads, own_keys, preferred_element_type=jnp.float32)
        * scale
    )
    tree_scores = jnp.where(tree_mask[:, None, None, :], tree_scores, NEGATIVE)
    local_top = jnp.maximum(
        jnp.max(stored_scores, axis=-1).reshape(all_rows, KV_HEADS, groups),
        jnp.max(tree_scores, axis=-1),
    )
    top = lax.pmax(local_top, "tp")
    top_blocks = top.reshape(requests, tree, KV_HEADS, groups)

    def cache_mix(items):
        block_scores, block_top, values = items
        exponent = jnp.exp(block_scores - block_top[..., None])
        block_totals = jnp.sum(exponent, axis=-1)
        block_mixed = jnp.einsum(
            "tkgp,pkd->tkgd",
            exponent.astype(jnp.bfloat16),
            values.reshape(places_dev, KV_HEADS, HEAD),
            preferred_element_type=jnp.float32,
        )
        return (block_mixed, block_totals)

    mixed, totals = lax.map(cache_mix, (stored_scores, top_blocks, cache_values))
    tree_exp = jnp.exp(tree_scores - top[..., None])
    mixed = mixed.reshape(all_rows, KV_HEADS, groups, HEAD) + jnp.einsum(
        "tkgu,ukd->tkgd",
        tree_exp.astype(jnp.bfloat16),
        own_values,
        preferred_element_type=jnp.float32,
    )
    totals = totals.reshape(all_rows, KV_HEADS, groups) + jnp.sum(tree_exp, axis=-1)
    totals_all = lax.psum(totals.reshape(all_rows, HEADS), "tp")
    mixed_cols = lax.psum_scatter(
        mixed.reshape(all_rows, model_width), "tp", scatter_dimension=1, tiled=True
    )
    columns = w_out.shape[0]
    column_head = (tp_rank * columns + jnp.arange(columns, dtype=jnp.int32)) // HEAD
    head_pick = (jnp.arange(HEADS, dtype=jnp.int32)[:, None] == column_head[None, :]).astype(
        jnp.float32
    )
    column_totals = jnp.dot(totals_all, head_pick, precision=lax.Precision.HIGHEST)
    attended = (mixed_cols / column_totals).astype(jnp.bfloat16)
    partial_terms = jnp.dot(attended, w_out, preferred_element_type=jnp.float32)
    projected = lax.psum_scatter(partial_terms, "tp", scatter_dimension=1, tiled=True)
    return (inputs + projected).astype(jnp.bfloat16)


def solution(mesh):
    placed = (
        P("req", "tp"),
        P("tp"),
        P("tp", None),
        P("tp", None),
        P("req", "tp", None),
        P("req", "tp", None),
        P("req", None),
        P("req"),
        P("req"),
    )
    return jax.shard_map(
        on_device, mesh=mesh, in_specs=placed, out_specs=P("req", "tp"), check_vma=False
    )
```

profile of v0, /device:TPU:2, one launch (start us, length us, event | category | flops | bytes accessed | tf_op | source)
XLA Modules:
  0.0 868.9 jit_solution(1173911116524621926)
XLA Ops:
  6.5 0.7 convert_element_type.75
  7.3 0.4 copy-done
  7.6 2.1 fusion.28
  9.8 0.8 fusion.24
  11.3 0.8 fusion.27
  13.1 132.0 %psum.22 = f32[64]{0:T(128)S(1)} all-reduce(f32[64]{0:T(128)S(1)} %fusion.24), channel_id=1, replica_groups=mesh['req'=4,'tp'=64] {'tp'}, use_global_device_ids=true, to_apply=%region_2.0 | all-reduce | flops 64 | bytes 512 | tf_op jit(solution)/shard_map/psum | solution.py:41
  145.8 1.3 reshape.297
  147.1 1.3 reshape.299
  148.8 54.3 %all-reduce.2.cloned.1.call-done = f32[64,5120]{1,0:T(8,128)} async-done(((f32[64,5120]{1,0:T(8,128)}), f32[64,5120]{1,0:T(8,128)}) %all-reduce.2.cloned.1.call-update) | async-done | bytes 1310736 | tf_op jit(solution)/shard_map/psum | solution.py:41
  203.1 1.5 multiply_convert_fusion
  204.7 2.4 fusion.19
  207.1 4.7 bitcast_reduce_fusion
  211.9 248.6 %pmax.7 = f32[64,4,8]{2,0,1:T(8,128)S(1)} all-reduce(f32[64,4,8]{2,0,1:T(8,128)S(1)} %bitcast_maximum_fusion), channel_id=1, replica_groups=mesh['req'=4,'tp'=64] {'tp'}, use_global_device_ids=true, to_apply=%region_4.5 | all-reduce | flops 2048 | bytes 16384 | tf_op jit(solution)/shard_map/pmax | solution.py:94
  460.5 0.7 convert_bitcast_fusion
  461.3 4.6 fusion.9
  466.0 2.0 copy.38
  468.1 4.5 fusion.1
  472.8 246.3 %psum.23 = f32[64,32]{0,1:T(8,128)S(1)} all-reduce(f32[64,32]{0,1:T(8,128)S(1)} %bitcast_add_fusion), channel_id=1, replica_groups=mesh['req'=4,'tp'=64] {'tp'}, use_global_device_ids=true, to_apply=%region_7.8 | all-reduce | flops 2048 | bytes 16384 | tf_op jit(solution)/shard_map/psum | solution.py:118
  719.1 0.8 copy.35
  719.9 0.2 fusion.12
  720.2 1.9 convolution_bitcast_fusion
  722.1 138.9 %reduce-scatter.9.cloned.1.call-done = f32[64,64]{1,0:T(8,128)} async-done(((f32[4096,64]{1,0:T(8,128)}), f32[64,64]{1,0:T(8,128)}) %reduce-scatter.9.cloned.1.call-update) | async-done | bytes 16400
  860.9 0.8 copy.37
  861.8 0.6 fusion.25
  (32 shorter events, 1.9 us)
Async XLA Ops:
  6.5 1.1 copy-start
  6.5 196.5 %all-reduce.2.cloned.1.call-start = ((), (), s32[]{:S(2)}) async-start(), calls=%async_computation.2 | async-start | bytes 2621440 | tf_op jit(solution)/shard_map/psum | solution.py:41
  9.8 709.3 %reduce-scatter.7.cloned.1.call-start = ((), (), s32[]{:S(2)}) async-start(), calls=%async_computation.3 | async-start | bytes 2129920
  466.0 6.7 copy-start.2
  466.0 254.1 %copy-start.1 = (bf16[64,4096]{1,0:T(8,128)(2,1)S(1)}, bf16[64,4096]{1,0:T(8,128)(2,1)}, u32[]{:S(2)}) copy-start(bf16[64,4096]{1,0:T(8,128)(2,1)} %param.12) | copy-start | bytes 1572868
  468.0 393.7 %copy-start.3 = (bf16[64,64]{1,0:T(8,128)(2,1)S(1)}, bf16[64,64]{1,0:T(8,128)(2,1)}, u32[]{:S(2)}) copy-start(bf16[64,64]{1,0:T(8,128)(2,1)} %param.9) | copy-start | bytes 24580
  468.1 392.9 %reduce-scatter.9.cloned.1.call-start = ((), (), s32[]{:S(2)}) async-start(), calls=%async_computation.4 | async-start | bytes 2129920
Sparse Core Ops, SparseCore 0:
  10.8 192.2 all-reduce.1
  468.2 138.6 reduce-scatter.6
  722.2 138.7 reduce-scatter.8
where the time goes:
time: 869 us
  blocking collectives  627 us (72%)
  waiting for transfers between devices  193 us (22%)
  matrix products  17.3 us (2%)
  between operations  14.6 us (2%)
  other arithmetic  9.83 us (1%)
    pmax x1, blocking collectives, on_device(): top = lax.pmax(local_top, 'tp')  249 us
    psum x1, blocking collectives, on_device(): totals_all = lax.psum(totals.reshape(all_rows, HEADS), 'tp')  246 us
    unnamed x5, waiting for transfers between devices  139 us
    psum x1, blocking collectives, on_device(): lax.psum((jnp.dot(scaled, w_qkv, preferred_element_type=jnp.float32), loc...  132 us
    psum x1, waiting for transfers between devices, on_device(): lax.psum((jnp.dot(scaled, w_qkv, preferred_element_type=jnp.float32), loc...  54.3 us
  transfers between devices with their start and end apart: 3, of which 2 were waited for; matrix products, arithmetic and copies ran while one was open for 1% of the time, Pallas kernels for 0%

commit v1 on v0

--- a/solution.py
+++ b/solution.py
@@ -115,7 +115,7 @@
         preferred_element_type=jnp.float32,
     )
     totals = totals.reshape(all_rows, KV_HEADS, groups) + jnp.sum(tree_exp, axis=-1)
-    totals_all = lax.psum(totals.reshape(all_rows, HEADS), "tp")
+    totals_all = jnp.sum(lax.all_gather(totals.reshape(all_rows, HEADS), "tp"), axis=0)
     mixed_cols = lax.psum_scatter(
         mixed.reshape(all_rows, model_width), "tp", scatter_dimension=1, tiled=True
     )

time: 869 us -> 759 us (0.87)
  blocking collectives: 627 us -> 428 us
  waiting for transfers between devices: 193 us -> 282 us
    psum x1 -> x0, blocking collectives: 246 us -> none  [on_device(): totals_all = lax.psum(totals.reshape(all_rows, HEADS), 'tp')]
    unnamed x5, waiting for transfers between devices: 139 us -> 228 us
    all_gather x0 -> x1, blocking collectives: none -> 47.2 us  [on_device(): lax.all_gather(totals.reshape(all_rows, HEADS), 'tp')]
  transfers between devices with their start and end apart: 3 -> 3, of which waited for: 2 -> 3; matrix products, arithmetic and copies ran while one was open for 1% -> 1% of each run, Pallas kernels for 0% -> 0%
where the time goes in v1:
time: 759 us
  blocking collectives  428 us (56%)
  waiting for transfers between devices  282 us (37%)
  matrix products  17.3 us (2%)
  between operations  14.6 us (2%)
  other arithmetic  9.93 us (1%)
    pmax x1, blocking collectives, on_device(): top = lax.pmax(local_top, 'tp')  249 us
    unnamed x5, waiting for transfers between devices  228 us
    psum x1, blocking collectives, on_device(): lax.psum((jnp.dot(scaled, w_qkv, preferred_element_type=jnp.float32), loc...  132 us
    psum x1, waiting for transfers between devices, on_device(): lax.psum((jnp.dot(scaled, w_qkv, preferred_element_type=jnp.float32), loc...  54.3 us
    all_gather x1, blocking collectives, on_device(): lax.all_gather(totals.reshape(all_rows, HEADS), 'tp')  47.2 us
  transfers between devices with their start and end apart: 3, of which 3 were waited for; matrix products, arithmetic and copies ran while one was open for 1% of the time, Pallas kernels for 0%

profile of v1, /device:TPU:2, one launch (start us, length us, event | category | flops | bytes accessed | tf_op | source)
XLA Modules:
  0.0 758.7 jit_solution(14692439131608582330)
XLA Ops:
  6.5 0.7 convert_element_type.75
  7.3 0.4 copy-done
  7.6 2.1 fusion.28
  9.8 0.8 fusion.24
  11.3 0.8 fusion.27
  13.1 132.0 %psum.15 = f32[64]{0:T(128)S(1)} all-reduce(f32[64]{0:T(128)S(1)} %fusion.24), channel_id=1, replica_groups=mesh['req'=4,'tp'=64] {'tp'}, use_global_device_ids=true, to_apply=%region_2.0 | all-reduce | flops 64 | bytes 512 | tf_op jit(solution)/shard_map/psum | solution.py:41
  145.8 1.3 reshape.311
  147.1 1.3 reshape.313
  148.8 54.3 %all-reduce.2.cloned.1.call-done = f32[64,5120]{1,0:T(8,128)} async-done(((f32[64,5120]{1,0:T(8,128)}), f32[64,5120]{1,0:T(8,128)}) %all-reduce.2.cloned.1.call-update) | async-done | bytes 1310736 | tf_op jit(solution)/shard_map/psum | solution.py:41
  203.1 1.5 multiply_convert_fusion
  204.7 2.4 fusion.19
  207.1 4.7 bitcast_reduce_fusion
  211.9 248.6 %pmax.7 = f32[64,4,8]{2,0,1:T(8,128)S(1)} all-reduce(f32[64,4,8]{2,0,1:T(8,128)S(1)} %bitcast_maximum_fusion), channel_id=1, replica_groups=mesh['req'=4,'tp'=64] {'tp'}, use_global_device_ids=true, to_apply=%region_4.5 | all-reduce | flops 2048 | bytes 16384 | tf_op jit(solution)/shard_map/pmax | solution.py:94
  460.5 0.7 convert_bitcast_fusion
  461.3 4.6 fusion.9
  466.0 2.0 copy.38
  468.2 4.5 fusion.1
  472.8 47.2 %all_gather.3 = f32[64,64,32]{1,2,0:T(8,128)S(1)} all-gather(f32[1,64,32]{1,2,0:T(8,128)S(1)} %bitcast_add_fusion), channel_id=1, replica_groups=mesh['req'=4,'tp'=64] {'tp'}, dimensions={0}, use_global_device_ids=true | all-gather | bytes 532480 | tf_op jit(solution)/shard_map/all_gather | solution.py:118
  520.1 86.8 %reduce-scatter.7.cloned.1.call-done = f32[64,64]{1,0:T(8,128)} async-done(((f32[4096,64]{1,0:T(8,128)}), f32[64,64]{1,0:T(8,128)}) %reduce-scatter.7.cloned.1.call-update) | async-done | bytes 16400
  606.9 0.8 copy.35
  607.9 1.9 convolution_bitcast_fusion
  609.9 140.9 %reduce-scatter.9.cloned.1.call-done = f32[64,64]{1,0:T(8,128)} async-done(((f32[4096,64]{1,0:T(8,128)}), f32[64,64]{1,0:T(8,128)}) %reduce-scatter.9.cloned.1.call-update) | async-done | bytes 16400
  750.7 0.8 copy.37
  751.6 0.6 fusion.25
  (33 shorter events, 2.2 us)
Async XLA Ops:
  6.5 1.1 copy-start
  6.5 196.5 %all-reduce.2.cloned.1.call-start = ((), (), s32[]{:S(2)}) async-start(), calls=%async_computation.2 | async-start | bytes 2621440 | tf_op jit(solution)/shard_map/psum | solution.py:41
  9.8 597.1 %reduce-scatter.7.cloned.1.call-start = ((), (), s32[]{:S(2)}) async-start(), calls=%async_computation.3 | async-start | bytes 2129920
  466.0 6.7 copy-start.2
  466.0 141.9 %copy-start.1 = (bf16[64,4096]{1,0:T(8,128)(2,1)S(1)}, bf16[64,4096]{1,0:T(8,128)(2,1)}, u32[]{:S(2)}) copy-start(bf16[64,4096]{1,0:T(8,128)(2,1)} %param.12) | copy-start | bytes 1572868
  468.1 283.5 %copy-start.3 = (bf16[64,64]{1,0:T(8,128)(2,1)S(1)}, bf16[64,64]{1,0:T(8,128)(2,1)}, u32[]{:S(2)}) copy-start(bf16[64,64]{1,0:T(8,128)(2,1)} %param.9) | copy-start | bytes 24580
  468.1 282.7 %reduce-scatter.9.cloned.1.call-start = ((), (), s32[]{:S(2)}) async-start(), calls=%async_computation.4 | async-start | bytes 2129920
Sparse Core Ops, SparseCore 0:
  10.8 192.2 all-reduce.1
  468.2 138.6 reduce-scatter.6
  610.9 139.7 reduce-scatter.8
